TPU v7x, 128 devices: a whole 4x4x4 slice. The times are simulated.
128 devices in a mesh: sector: 8 (over y, core), row: 16 (over x, z).
Axes of the slice: x: 4, y: 4, z: 4, core: 2. Of those that a mesh axis runs over, the one named last changes fastest.
Arguments:
- amplitudes: bfloat16 [8192, 4, 8192], P('sector', None, 'row'), may hold values from -6 to 6
- next_site: bfloat16 [8, 4, 8192, 2048], P('sector', None, 'row'), may hold values from -0.03125 to 0.03125
- sector_rows: int32 [8], replicated, may hold values from 512 to 1024, as said below
- moves: int32 [2, 8], replicated, may hold values from 0 to 128, as said below
- angles: float32 [2, 8, 128], replicated, may hold values from -3.140625 to 3.140625
- ranks: int32 [8], replicated, may hold values from 256 to 1024, as said below
Outputs:
- canonical: bfloat16 [2048, 8192], P('row', 'sector')
Inputs may be any that keep to these rules, and one draw needn't show every extreme that they name: `sector_rows`: one sector has exactly 1024 live rows and another exactly 512. `moves`: the entry of the last sector is 0, every other entry is 1 or more; for each gate some pair moves exactly 128 rows. `ranks`: each sector keeps at least half of its live rows and at most all of them; one sector keeps 1024 rows and one keeps 1024 // 4.
All inputs are finite; a program needn't handle non-finite values.
Results may differ from a plain program's by a relative error of at most 0.014.
Values may be sent and summed in bfloat16 or wider, within the bound.
No kernel may reach another device: no remote copies, remote signals or barrier semaphores. Data moves between devices by JAX's collectives and lax.ppermute only.
A program may use at most 128 MiB of HBM per device.

v0:
```python
import math
import jax
import jax.numpy as jnp
from jax import lax
from jax.sharding import PartitionSpec as P

KOUT = 2048
BLOCK = 128
HI = lax.Precision.HIGHEST


def shifted(x, axis, by):
    size = lax.axis_size(axis)
    pairs = [(i, i + by) for i in range(size) if 0 <= i + by < size]
    return lax.ppermute(x, axis, pairs)


def rotated_window(own, partner, angle, count, sign):
    slot_index = jnp.arange(own.shape[0])
    own32 = own.astype(jnp.float32)
    partner32 = partner.astype(jnp.float32)
    cos_t = jnp.cos(angle)[:, None, None]
    sin_t = jnp.sin(angle)[:, None, None]
    if sign < 0:
        new = cos_t * own32 - sin_t * partner32
    else:
        new = sin_t * partner32 + cos_t * own32
    return jnp.where((slot_index < count)[:, None, None], new, own32).astype(jnp.bfloat16)


def dot(a, b):
    return jnp.dot(a, b, precision=HI, preferred_element_type=jnp.float32)


def cholesky_solve(gram, rhs):
    n = gram.shape[0]
    eye = jnp.eye(BLOCK, dtype=jnp.float32)
    trailing = gram
    rest = rhs
    solved = []
    for start in range(0, n, BLOCK):
        diag = trailing[:BLOCK, :BLOCK]
        factor = jnp.linalg.cholesky(diag)
        inverse = lax.linalg.triangular_solve(factor, eye, left_side=True, lower=True)
        head = dot(inverse, rest[:BLOCK])
        solved.append(head)
        if start + BLOCK < n:
            panel = lax.dot_general(
                trailing[BLOCK:, :BLOCK],
                inverse,
                (((1,), (1,)), ((), ())),
                precision=HI,
                preferred_element_type=jnp.float32,
            )
            trailing = trailing[BLOCK:, BLOCK:] - lax.dot_general(
                panel,
                panel,
                (((1,), (1,)), ((), ())),
                precision=HI,
                preferred_element_type=jnp.float32,
            )
            rest = rest[BLOCK:] - dot(panel, head)
    return jnp.concatenate(solved, 0)


def per_device(amplitudes, next_site, sector_rows, moves, angles, ranks):
    sector_id = lax.axis_index("sector")
    rows = amplitudes.shape[0]
    move_rows = angles.shape[-1]
    row_index = jnp.arange(rows)
    live_rows = sector_rows[sector_id]
    prev_id = jnp.maximum(sector_id - 1, 0)
    count_here = moves[:, sector_id]
    count_prev = jnp.where(sector_id > 0, moves[:, prev_id], 0)
    masked = jnp.where(
        (row_index < live_rows)[:, None, None], amplitudes, jnp.zeros((), amplitudes.dtype)
    )
    padded = jnp.concatenate([masked, jnp.zeros((move_rows,) + masked.shape[1:], masked.dtype)], 0)
    starts_a = [live_rows - count_here[0], live_rows - count_here[0] - count_here[1]]
    starts_b = [jnp.int32(0), count_prev[0]]
    own_a = [lax.dynamic_slice_in_dim(padded, s, move_rows, 0) for s in starts_a]
    own_b = [lax.dynamic_slice_in_dim(padded, s, move_rows, 0) for s in starts_b]
    from_below = [shifted(w, "sector", 1) for w in own_a]
    from_above = [shifted(w, "sector", -1) for w in own_b]
    new_a = [
        rotated_window(own_a[g], from_above[g], angles[g][sector_id], count_here[g], -1)
        for g in range(2)
    ]
    new_b = [
        rotated_window(own_b[g], from_below[g], angles[g][prev_id], count_prev[g], 1)
        for g in range(2)
    ]
    padded = lax.dynamic_update_slice_in_dim(padded, new_a[1], starts_a[1], 0)
    padded = lax.dynamic_update_slice_in_dim(padded, new_a[0], starts_a[0], 0)
    padded = lax.dynamic_update_slice_in_dim(padded, new_b[0], starts_b[0], 0)
    padded = lax.dynamic_update_slice_in_dim(padded, new_b[1], starts_b[1], 0)
    block_rows = padded[:rows]
    site_tensor = next_site[0]
    contracted = lax.psum_scatter(
        jnp.einsum("prk,lpr->kl", site_tensor, block_rows, preferred_element_type=jnp.float32),
        "row",
        scatter_dimension=0,
        tiled=True,
    ).astype(jnp.bfloat16)
    gathered = lax.all_gather(contracted, "row", axis=0, tiled=True)
    gram_matrix = lax.dot_general(
        gathered, gathered, (((0,), (0,)), ((), ())), preferred_element_type=jnp.float32
    )
    dead_rows = (row_index >= live_rows).astype(jnp.float32)
    gram_matrix = gram_matrix + jnp.diag(dead_rows)
    solved = cholesky_solve(gram_matrix, contracted.astype(jnp.float32).T).T
    kept_mask = ((row_index >= live_rows - ranks[sector_id]) & (row_index < live_rows)).astype(
        jnp.float32
    )
    return (solved * math.sqrt(KOUT) * kept_mask[None, :]).astype(jnp.bfloat16)


def solution(mesh):
    placed = (P("sector", None, "row"), P("sector", None, "row", None), P(), P(), P(), P())
    return jax.shard_map(
        per_device, mesh=mesh, in_specs=placed, out_specs=P("row", "sector"), check_vma=False
    )
```

profile of v0, /device:TPU:0, one launch (start us, length us, event | category | flops | bytes accessed | tf_op | source)
XLA Modules:
  0.0 469.1 jit_solution(3784771538041529058)
XLA Ops:
  6.5 1.3 dynamic_slice.36
  11.8 5.1 %copy_select_fusion = bf16[1024,4,512]{2,0,1:T(8,128)(2,1)S(1)} fusion(bf16[1024,4,512]{2,1,0:T(4,128)(2,1)} %param.9, pred[1024]{0:T(1024)(128)(4,1)S(1)} %iota_compare_fusion.13), kind=kLoop, calls=%fused_computation.4 | loop fusion | flops 2097152 | bytes 8389632 | tf_op jit(solution)/shard_map/jit(_where)/select_n | solution.py:75
  16.9 1.9 copy-done
  19.0 1.3 collective-permute-start.1
  20.3 3.1 collective-permute-start.3
  27.2 2.0 fusion.9
  29.1 1.3 collective-permute-start
  30.4 6.1 %collective-permute-start.2 = (bf16[128,4,512]{2,0,1:T(8,128)(2,1)S(1)}, bf16[128,4,512]{2,0,1:T(8,128)(2,1)S(1)}, u32[]{:S(2)}, u32[]{:S(2)}) collective-permute-start(bf16[128,4,512]{2,0,1:T(8,128)(2,1)S(1)} %get-tuple-element.10), channel_id=1, source_target_pairs={{0,16},{16,32},{32,48},{48,64},{64,80},{80,96},{96,112},{1,17},{17... | collective-permute-start | bytes 1572872 | tf_op jit(solution)/shard_map/ppermute | solution.py:15
  36.6 2.5 concatenate.6
  40.7 5.6 %dynamic_update_slice.12 = bf16[1152,4,512]{2,0,1:T(8,128)(2,1)} dynamic-update-slice(bf16[1152,4,512]{2,0,1:T(8,128)(2,1)} %concatenate.6, bf16[128,4,512]{2,0,1:T(8,128)(2,1)S(1)} %fusion.7, s32[]{:T(128)S(6)} %select_n.58, s32[]{:T(128)} %constant.51.clone.1, s32[]{:T(128)} %constant.51.clone.1) | dynamic-update-slice | bytes 1048580 | tf_op jit(solution)/shard_map/dynamic_update_slice | solution.py:93
  46.2 5.6 %dynamic_update_slice.13 = bf16[1152,4,512]{2,0,1:T(8,128)(2,1)} dynamic-update-slice(bf16[1152,4,512]{2,0,1:T(8,128)(2,1)} %dynamic_update_slice.12, bf16[128,4,512]{2,0,1:T(8,128)(2,1)S(1)} %get-tuple-element.9, s32[]{:T(128)S(6)} %select_n.63, s32[]{:T(128)} %constant.51.clone.1, s32[]{:T(128)} %constant.51.clone.1) | dynamic-update-slice | bytes 1048580 | tf_op jit(solution)/shard_map/dynamic_update_slice | solution.py:94
  51.8 2.2 fusion.14
  54.0 5.5 %dynamic_update_slice.15 = bf16[1152,4,512]{2,0,1:T(8,128)(2,1)} dynamic-update-slice(bf16[1152,4,512]{2,0,1:T(8,128)(2,1)} %fusion.14, bf16[128,4,512]{2,0,1:T(8,128)(2,1)S(1)} %get-tuple-element.11, s32[]{:T(128)S(6)} %select_n.61, s32[]{:T(128)} %constant.51.clone.1, s32[]{:T(128)} %constant.51.clone.1) | dynamic-update-slice | bytes 1048580 | tf_op jit(solution)/shard_map/dynamic_update_slice | solution.py:96
  59.5 14.4 %fusion.2 = f32[2048,1024]{0,1:T(8,128)} fusion(bf16[1,4,512,2048]{3,2,1,0:T(8,128)(2,1)} %param.10, bf16[1152,4,512]{2,0,1:T(8,128)(2,1)} %dynamic_update_slice.15), kind=kOutput, calls=%fused_computation.2 | convolution fusion | flops 8589934592 | bytes 20971520 | tf_op jit(solution)/shard_map/prk,lpr->kl/dot_general | solution.py:100
  74.0 90.8 %reduce-scatter.2.cloned.1.call-done = f32[128,1024]{0,1:T(8,128)} async-done(((f32[2048,1024]{0,1:T(8,128)}), f32[128,1024]{0,1:T(8,128)}) %reduce-scatter.2.cloned.1.call-update) | async-done | bytes 524304 | tf_op jit(solution)/shard_map/reduce_scatter | solution.py:99
  164.9 1.8 convert_element_type.87
  169.7 1.1 convert_bitcast_fusion
  170.8 53.2 %all-gather.2.cloned.1.call-done = bf16[2048,1024]{0,1:T(8,128)(2,1)} async-done(((bf16[128,1024]{0,1:T(8,128)(2,1)}), bf16[2048,1024]{0,1:T(8,128)(2,1)}) %all-gather.2.cloned.1.call-update) | async-done | bytes 4194320 | tf_op jit(solution)/shard_map/all_gather | solution.py:105
  224.0 8.6 %select_add_fusion = f32[1024,1024]{0,1:T(8,128)S(1)} fusion(f32[1024]{0:T(1024)S(1)} %fusion.84, bf16[2048,1024]{0,1:T(8,128)(2,1)} %all-gather.2.cloned.1.call-done), kind=kOutput, calls=%fused_computation.5 | convolution fusion | flops 4298113024 | bytes 8392704 | tf_op jit(solution)/shard_map/dot_general | solution.py:106
  232.6 1.9 copy-done.8
  235.5 11.7 %cholesky.134 = f32[128,128]{1,0:T(8,128)S(1)} custom-call(f32[128,128]{1,0:T(8,128)S(1)} %fusion.81), custom_call_target="Cholesky" | custom-call | tf_op jit(solution)/shard_map/jit(cholesky)/cholesky | solution.py:43
  248.6 9.8 %custom-call.12 = f32[1,128,128]{1,2,0:T(8,128)S(1)} custom-call(f32[1,128,128]{2,1,0:T(8,128)S(1)} %fusion.44), custom_call_target="InvertDiagBlocksLowerTriangular" | custom-call | tf_op jit(solution)/shard_map/triangular_solve/custom-call.0 | solution.py:44
  259.3 1.9 fusion.15
  262.0 4.6 slice_subtract_fusion
  268.8 12.7 %cholesky.145 = f32[128,128]{1,0:T(8,128)S(1)} custom-call(f32[128,128]{1,0:T(8,128)} %fusion.79), custom_call_target="Cholesky" | custom-call | tf_op jit(solution)/shard_map/jit(cholesky)/cholesky | solution.py:43
  282.2 1.2 fusion.45
  283.4 10.6 %custom-call.13 = f32[1,128,128]{1,2,0:T(8,128)S(1)} custom-call(f32[1,128,128]{2,1,0:T(8,128)} %fusion.45), custom_call_target="InvertDiagBlocksLowerTriangular" | custom-call | tf_op jit(solution)/shard_map/triangular_solve/custom-call.0 | solution.py:44
  295.8 2.0 slice_subtract_fusion.1
  297.9 1.4 copy-done.2
  300.2 11.7 %cholesky.156 = f32[128,128]{1,0:T(8,128)S(1)} custom-call(f32[128,128]{1,0:T(8,128)S(1)} %fusion.77), custom_call_target="Cholesky" | custom-call | tf_op jit(solution)/shard_map/jit(cholesky)/cholesky | solution.py:43
  313.3 10.0 %custom-call.14 = f32[1,128,128]{1,2,0:T(8,128)S(1)} custom-call(f32[1,128,128]{2,1,0:T(8,128)S(1)} %fusion.46), custom_call_target="InvertDiagBlocksLowerTriangular" | custom-call | tf_op jit(solution)/shard_map/triangular_solve/custom-call.0 | solution.py:44
  323.6 1.7 fusion.19
  325.3 2.9 slice_subtract_fusion.2
  328.3 11.7 %cholesky.167 = f32[128,128]{1,0:T(8,128)S(1)} custom-call(f32[128,128]{1,0:T(8,128)S(1)} %fusion.75), custom_call_target="Cholesky" | custom-call | tf_op jit(solution)/shard_map/jit(cholesky)/cholesky | solution.py:43
  341.5 9.8 %custom-call.15 = f32[1,128,128]{1,2,0:T(8,128)S(1)} custom-call(f32[1,128,128]{2,1,0:T(8,128)S(1)} %fusion.47), custom_call_target="InvertDiagBlocksLowerTriangular" | custom-call | tf_op jit(solution)/shard_map/triangular_solve/custom-call.0 | solution.py:44
  352.2 1.0 convolution_subtract_fusion
  355.2 12.1 %cholesky.178 = f32[128,128]{1,0:T(8,128)S(1)} custom-call(f32[128,128]{1,0:T(8,128)S(1)} %fusion.73), custom_call_target="Cholesky" | custom-call | tf_op jit(solution)/shard_map/jit(cholesky)/cholesky | solution.py:43
  368.8 9.8 %custom-call.16 = f32[1,128,128]{1,2,0:T(8,128)S(1)} custom-call(f32[1,128,128]{2,1,0:T(8,128)S(1)} %fusion.48), custom_call_target="InvertDiagBlocksLowerTriangular" | custom-call | tf_op jit(solution)/shard_map/triangular_solve/custom-call.0 | solution.py:44
  378.9 1.4 fusion.40
  380.3 1.7 convolution_subtract_fusion.1
  382.1 11.7 %cholesky.189 = f32[128,128]{1,0:T(8,128)S(1)} custom-call(f32[128,128]{1,0:T(8,128)S(1)} %fusion.71), custom_call_target="Cholesky" | custom-call | tf_op jit(solution)/shard_map/jit(cholesky)/cholesky | solution.py:43
  395.3 9.8 %custom-call.17 = f32[1,128,128]{1,2,0:T(8,128)S(1)} custom-call(f32[1,128,128]{2,1,0:T(8,128)S(1)} %fusion.49), custom_call_target="InvertDiagBlocksLowerTriangular" | custom-call | tf_op jit(solution)/shard_map/triangular_solve/custom-call.0 | solution.py:44
  407.1 11.7 %cholesky.200 = f32[128,128]{1,0:T(8,128)S(1)} custom-call(f32[128,128]{1,0:T(8,128)S(1)} %fusion.69), custom_call_target="Cholesky" | custom-call | tf_op jit(solution)/shard_map/jit(cholesky)/cholesky | solution.py:43
  420.0 9.8 %custom-call.18 = f32[1,128,128]{1,2,0:T(8,128)S(1)} custom-call(f32[1,128,128]{2,1,0:T(8,128)S(1)} %fusion.50), custom_call_target="InvertDiagBlocksLowerTriangular" | custom-call | tf_op jit(solution)/shard_map/triangular_solve/custom-call.0 | solution.py:44
  432.0 1.0 constant_dynamic-update-slice_fusion.5
  433.5 1.0 constant_dynamic-update-slice_fusion.4
  437.4 11.9 %cholesky.211 = f32[128,128]{1,0:T(8,128)S(1)} custom-call(f32[128,128]{1,0:T(8,128)S(1)} %fusion.67), custom_call_target="Cholesky" | custom-call | tf_op jit(solution)/shard_map/jit(cholesky)/cholesky | solution.py:43
  450.7 9.8 %custom-call.19 = f32[1,128,128]{1,2,0:T(8,128)S(1)} custom-call(f32[1,128,128]{2,1,0:T(8,128)S(1)} %fusion.51), custom_call_target="InvertDiagBlocksLowerTriangular" | custom-call | tf_op jit(solution)/shard_map/triangular_solve/custom-call.0 | solution.py:44
  (126 shorter events, 37.6 us)
Async XLA Ops:
  6.5 158.3 %reduce-scatter.2.cloned.1.call-start = ((), (), s32[]{:S(2)}) async-start(), calls=%async_computation.1 | async-start | bytes 8912896 | tf_op jit(solution)/shard_map/reduce_scatter | solution.py:99
  16.9 1.9 copy-start
  18.8 8.2 %copy-start.14 = (f32[2,8,128]{2,1,0:T(8,128)S(1)}, f32[2,8,128]{2,1,0:T(8,128)}, u32[]{:S(2)}) copy-start(f32[2,8,128]{2,1,0:T(8,128)} %param.13) | copy-start | bytes 24580
  19.0 8.1 %collective-permute-start.1 = (bf16[128,4,512]{2,0,1:T(8,128)(2,1)S(1)}, bf16[128,4,512]{2,0,1:T(8,128)(2,1)S(1)}, u32[]{:S(2)}, u32[]{:S(2)}) collective-permute-start(bf16[128,4,512]{2,0,1:T(8,128)(2,1)S(1)} %get-tuple-element.13), channel_id=1, source_target_pairs={{16,0},{32,16},{48,32},{64,48},{80,64},{96,80},{112,96},{17,1},{33... | collective-permute-start | bytes 1572872 | tf_op jit(solution)/shard_map/ppermute | solution.py:15
  20.3 6.8 %collective-permute-start.3 = (bf16[128,4,512]{2,0,1:T(8,128)(2,1)S(1)}, bf16[128,4,512]{2,0,1:T(8,128)(2,1)S(1)}, u32[]{:S(2)}, u32[]{:S(2)}) collective-permute-start(bf16[128,4,512]{2,0,1:T(8,128)(2,1)S(1)} %get-tuple-element.14), channel_id=1, source_target_pairs={{0,16},{16,32},{32,48},{48,64},{64,80},{80,96},{96,112},{1,17},{17... | collective-permute-start | bytes 1572872 | tf_op jit(solution)/shard_map/ppermute | solution.py:15
  25.4 11.2 %copy-start.1 = (bf16[1024,4,512]{2,0,1:T(8,128)(2,1)S(1)}, bf16[1024,4,512]{2,0,1:T(8,128)(2,1)}, u32[]{:S(2)}) copy-start(bf16[1024,4,512]{2,0,1:T(8,128)(2,1)} %copy-done) | copy-start | bytes 12582916
  29.1 11.2 %collective-permute-start = (bf16[128,4,512]{2,0,1:T(8,128)(2,1)S(1)}, bf16[128,4,512]{2,0,1:T(8,128)(2,1)S(1)}, u32[]{:S(2)}, u32[]{:S(2)}) collective-permute-start(bf16[128,4,512]{2,0,1:T(8,128)(2,1)S(1)} %get-tuple-element.12), channel_id=1, source_target_pairs={{16,0},{32,16},{48,32},{64,48},{80,64},{96,80},{112,96},{17,1},{33... | collective-permute-start | bytes 1572872 | tf_op jit(solution)/shard_map/ppermute | solution.py:15
  30.4 21.4 %collective-permute-start.2 = (bf16[128,4,512]{2,0,1:T(8,128)(2,1)S(1)}, bf16[128,4,512]{2,0,1:T(8,128)(2,1)S(1)}, u32[]{:S(2)}, u32[]{:S(2)}) collective-permute-start(bf16[128,4,512]{2,0,1:T(8,128)(2,1)S(1)} %get-tuple-element.10), channel_id=1, source_target_pairs={{0,16},{16,32},{32,48},{48,64},{64,80},{80,96},{96,112},{1,17},{17... | collective-permute-start | bytes 1572872 | tf_op jit(solution)/shard_map/ppermute | solution.py:15
  73.9 92.7 %copy-start.15 = (s32[8]{0:T(128)S(1)}, s32[8]{0:T(128)}, u32[]{:S(2)}) copy-start(s32[8]{0:T(128)} %param.14) | copy-start | bytes 100
  74.0 150.0 %all-gather.2.cloned.1.call-start = ((), (), s32[]{:S(2)}) async-start(), calls=%async_computation.2 | async-start | bytes 4456448 | tf_op jit(solution)/shard_map/all_gather | solution.py:105
  232.6 1.9 copy-start.8
  258.7 0.6 copy-start.13
  261.2 0.8 copy-start.3
  294.4 0.6 copy-start.11
  295.8 2.1 copy-start.5
  297.9 1.4 copy-start.2
  323.6 27.7 %copy-start.12 = (f32[128,128]{1,0:T(8,128)}, f32[128,128]{1,0:T(8,128)S(1)}, u32[]{:S(2)}) copy-start(f32[128,128]{1,0:T(8,128)S(1)} %fusion.34) | copy-start | bytes 196612
  352.2 79.3 %copy-start.4 = (f32[896,128]{1,0:T(8,128)S(1)}, f32[896,128]{1,0:T(8,128)}, u32[]{:S(2)}) copy-start(f32[896,128]{1,0:T(8,128)} %copy-done.3) | copy-start | bytes 1376260
  353.2 1.0 copy-start.7
  354.2 78.8 %copy-start.6 = (f32[768,128]{1,0:T(8,128)S(1)}, f32[768,128]{1,0:T(8,128)}, u32[]{:S(2)}) copy-start(f32[768,128]{1,0:T(8,128)} %copy-done.5) | copy-start | bytes 1179652
  405.4 0.6 copy-start.9
  406.9 29.2 %copy-start.10 = (f32[128,128]{1,0:T(8,128)S(1)}, f32[128,128]{1,0:T(8,128)}, u32[]{:S(2)}) copy-start(f32[128,128]{1,0:T(8,128)} %copy-done.9) | copy-start | bytes 196612
Sparse Core Ops, SparseCore 0:
  74.1 90.7 reduce-scatter.1
  167.0 56.9 all-gather.1
where the time goes:
time: 478 us; the launch traced here: 469 us
  other arithmetic  208 us (44%)
  waiting for transfers between devices  144 us (30%)
  matrix products  52 us (11%)
  local copies, waits for them, and re-layouts  33.9 us (7%)
  between operations  19.6 us (4%)
  starting transfers between devices  11.8 us (2%)
    another operation x24, other arithmetic, cholesky_solve(): factor = jnp.linalg.cholesky(diag)  101 us
    reduce_scatter x1, waiting for transfers between devices, per_device(): lax.psum_scatter(jnp.einsum('prk,lpr->kl', site_tensor, block_rows, prefe...  90.8 us
    another operation x16, other arithmetic, cholesky_solve(): lax.linalg.triangular_solve(factor, eye, left_side=True, lower=True)  85.3 us
    all_gather x1, waiting for transfers between devices, per_device(): gathered = lax.all_gather(contracted, 'row', axis=0, tiled=True)  53.2 us
    dot_general x1, matrix products, per_device(): jnp.einsum('prk,lpr->kl', site_tensor, block_rows, preferred_element_type...  14.4 us
    dot_general x7, matrix products, cholesky_solve(): lax.dot_general(panel, panel, (((1,), (1,)), ((), ())), precision=HI, pre...  12.9 us
    ppermute x4, starting transfers between devices, shifted(): return lax.ppermute(x, axis, pairs)  11.8 us
  transfers between devices with their start and end apart: 6, of which 2 were waited for; matrix products, arithmetic and copies ran while one was open for 4% of the time, Pallas kernels for 0%

commit v1 on v0

--- a/solution.py
+++ b/solution.py
@@ -7,6 +7,32 @@
 KOUT = 2048
 BLOCK = 128
 HI = lax.Precision.HIGHEST
+
+
+def switch_the_sector(incoming_x, dimension_no):
+    x_next = list(incoming_x.shape[1:])
+    x_next[dimension_no] *= incoming_x.shape[0]
+    q_next = jnp.moveaxis(incoming_x, 0, dimension_no).reshape(x_next)
+    return q_next
+
+
+def numbers_close(buf, named_axis, dim_at=0):
+    nd = lax.axis_size(named_axis)
+    found = [(m, (m + 1) % nd) for m in range(nd)]
+    known, earlier = ([], [])
+    leaves = [(to_i, tick) for tick, to_i in found]
+    hop_no = 0
+    while hop_no < nd - 1:
+        if hop_no % 2 == 0:
+            known.append(lax.ppermute(known[-1] if known else buf, named_axis, found))
+        else:
+            earlier.append(lax.ppermute(earlier[-1] if earlier else buf, named_axis, leaves))
+        hop_no += 1
+    mid_arr = jnp.stack([*known[::-1], buf, *earlier], axis=0)
+    work_now = lax.axis_index(named_axis) - len(known)
+    mid_arr = mid_arr[(jnp.arange(nd) - work_now) % nd]
+    z = switch_the_sector(mid_arr, dim_at)
+    return z
 
 
 def shifted(x, axis, by):
@@ -102,7 +128,7 @@
         scatter_dimension=0,
         tiled=True,
     ).astype(jnp.bfloat16)
-    gathered = lax.all_gather(contracted, "row", axis=0, tiled=True)
+    gathered = numbers_close(contracted, "row")
     gram_matrix = lax.dot_general(
         gathered, gathered, (((0,), (0,)), ((), ())), preferred_element_type=jnp.float32
     )

time: 478 us -> 527 us (1.10)
  starting transfers between devices: 11.8 us -> 51.7 us
  local copies, waits for them, and re-layouts: 33.9 us -> 50.6 us
  waiting for transfers between devices: 144 us -> 131 us
    all_gather x1 -> x0, waiting for transfers between devices: 53.2 us -> none  [per_device(): gathered = lax.all_gather(contracted, 'row', axis=0, tiled=True)]
    ppermute x0 -> x15, waiting for transfers between devices: none -> 40.1 us  [the longest x8 40.1 us: numbers_close(): known.append(lax.ppermute(known[-1] if known else buf, named_axis, found))]
    ppermute x0 -> x15, starting transfers between devices: none -> 39.7 us  [the longest x7 38.2 us: numbers_close(): lax.ppermute(earlier[-1] if earlier else buf, named_axis, leaves)]
    unnamed x32 -> x48, local copies, waits for them, and re-layouts: 8.85 us -> 19.6 us
  transfers between devices with their start and end apart: 6 -> 20, of which waited for: 2 -> 9; matrix products, arithmetic and copies ran while one was open for 4% -> 6% of each run, Pallas kernels for 0% -> 0%
where the time goes in v1:
time: 527 us; the launch traced here: 517 us
  other arithmetic  209 us (40%)
  waiting for transfers between devices  131 us (25%)
  matrix products  54.6 us (10%)
  starting transfers between devices  51.7 us (10%)
  local copies, waits for them, and re-layouts  50.6 us (10%)
  between operations  19.8 us (4%)
    another operation x24, other arithmetic, cholesky_solve(): factor = jnp.linalg.cholesky(diag)  101 us
    reduce_scatter x1, waiting for transfers between devices, per_device(): lax.psum_scatter(jnp.einsum('prk,lpr->kl', site_tensor, block_rows, prefe...  91 us
    another operation x16, other arithmetic, cholesky_solve(): lax.linalg.triangular_solve(factor, eye, left_side=True, lower=True)  85.8 us
    ppermute x8, waiting for transfers between devices, numbers_close(): known.append(lax.ppermute(known[-1] if known else buf, named_axis, found))  40.1 us
    ppermute x7, starting transfers between devices, numbers_close(): lax.ppermute(earlier[-1] if earlier else buf, named_axis, leaves)  38.2 us
    unnamed x48, local copies, waits for them, and re-layouts  19.6 us
    dot_general x1, matrix products, per_device(): jnp.einsum('prk,lpr->kl', site_tensor, block_rows, preferred_element_type...  14.5 us
    dot_general x7, matrix products, cholesky_solve(): lax.dot_general(panel, panel, (((1,), (1,)), ((), ())), precision=HI, pre...  12.9 us
  transfers between devices with their start and end apart: 20, of which 9 were waited for; matrix products, arithmetic and copies ran while one was open for 6% of the time, Pallas kernels for 0%

profile of v1, /device:TPU:0, one launch (start us, length us, event | category | flops | bytes accessed | tf_op | source)
XLA Modules:
  0.0 516.6 jit_solution(8982979294557651609)
XLA Ops:
  11.7 5.1 copy_select_fusion
  16.8 1.9 copy-done
  20.3 3.1 collective-permute-start.3
  26.9 2.0 fusion.9
  30.1 6.3 %collective-permute-start.2 = (bf16[128,4,512]{2,0,1:T(8,128)(2,1)S(1)}, bf16[128,4,512]{2,0,1:T(8,128)(2,1)S(1)}, u32[]{:S(2)}, u32[]{:S(2)}) collective-permute-start(bf16[128,4,512]{2,0,1:T(8,128)(2,1)S(1)} %get-tuple-element.10), channel_id=1, source_target_pairs={{0,16},{16,32},{32,48},{48,64},{64,80},{80,96},{96,112},{1,17},{17... | collective-permute-start | bytes 1572872 | tf_op jit(solution)/shard_map/ppermute | solution.py:41
  36.5 2.5 concatenate.6
  40.7 5.6 %dynamic_update_slice.12 = bf16[1152,4,512]{2,0,1:T(8,128)(2,1)} dynamic-update-slice(bf16[1152,4,512]{2,0,1:T(8,128)(2,1)} %concatenate.6, bf16[128,4,512]{2,0,1:T(8,128)(2,1)S(1)} %fusion.7, s32[]{:T(128)S(6)} %select_n.82, s32[]{:T(128)} %constant.68.clone.1, s32[]{:T(128)} %constant.68.clone.1) | dynamic-update-slice | bytes 1048580 | tf_op jit(solution)/shard_map/dynamic_update_slice | solution.py:119
  46.3 5.5 %dynamic_update_slice.13 = bf16[1152,4,512]{2,0,1:T(8,128)(2,1)} dynamic-update-slice(bf16[1152,4,512]{2,0,1:T(8,128)(2,1)} %dynamic_update_slice.12, bf16[128,4,512]{2,0,1:T(8,128)(2,1)S(1)} %get-tuple-element.9, s32[]{:T(128)S(6)} %select_n.87, s32[]{:T(128)} %constant.68.clone.1, s32[]{:T(128)} %constant.68.clone.1) | dynamic-update-slice | bytes 1048580 | tf_op jit(solution)/shard_map/dynamic_update_slice | solution.py:120
  51.8 2.2 fusion.14
  54.0 5.5 %dynamic_update_slice.15 = bf16[1152,4,512]{2,0,1:T(8,128)(2,1)} dynamic-update-slice(bf16[1152,4,512]{2,0,1:T(8,128)(2,1)} %fusion.14, bf16[128,4,512]{2,0,1:T(8,128)(2,1)S(1)} %get-tuple-element.11, s32[]{:T(128)S(6)} %select_n.85, s32[]{:T(128)} %constant.68.clone.1, s32[]{:T(128)} %constant.68.clone.1) | dynamic-update-slice | bytes 1048580 | tf_op jit(solution)/shard_map/dynamic_update_slice | solution.py:122
  59.5 14.5 %fusion.2 = f32[2048,1024]{0,1:T(8,128)} fusion(bf16[1,4,512,2048]{3,2,1,0:T(8,128)(2,1)} %param.10, bf16[1152,4,512]{2,0,1:T(8,128)(2,1)} %dynamic_update_slice.15), kind=kOutput, calls=%fused_computation.3 | convolution fusion | flops 8589934592 | bytes 20971520 | tf_op jit(solution)/shard_map/prk,lpr->kl/dot_general | solution.py:126
  74.0 91.0 %reduce-scatter.2.cloned.1.call-done = f32[128,1024]{0,1:T(8,128)} async-done(((f32[2048,1024]{0,1:T(8,128)}), f32[128,1024]{0,1:T(8,128)}) %reduce-scatter.2.cloned.1.call-update) | async-done | bytes 524304 | tf_op jit(solution)/shard_map/reduce_scatter | solution.py:125
  167.7 8.7 %collective-permute-done.4 = bf16[128,1024]{0,1:T(8,128)(2,1)S(1)} collective-permute-done((bf16[128,1024]{0,1:T(8,128)(2,1)S(1)}, bf16[128,1024]{0,1:T(8,128)(2,1)S(1)}, u32[]{:S(2)}, u32[]{:S(2)}) %collective-permute-start.4) | collective-permute-done | bytes 262176 | tf_op jit(solution)/shard_map/ppermute | solution.py:27
  176.4 5.3 %collective-permute-start.12 = (bf16[128,1024]{0,1:T(8,128)(2,1)S(1)}, bf16[128,1024]{0,1:T(8,128)(2,1)S(1)}, u32[]{:S(2)}, u32[]{:S(2)}) collective-permute-start(bf16[128,1024]{0,1:T(8,128)(2,1)S(1)} %convert_element_type.87), channel_id=1, source_target_pairs={{1,0},{2,1},{3,2},{4,3},{5,4},{6,5},{7,6},{8,7},{9,8},{10,9},{11,1... | collective-permute-start | bytes 786440 | tf_op jit(solution)/shard_map/ppermute | solution.py:29
  181.8 4.3 collective-permute-done.5
  186.1 5.3 %collective-permute-start.13 = (bf16[128,1024]{0,1:T(8,128)(2,1)S(1)}, bf16[128,1024]{0,1:T(8,128)(2,1)S(1)}, u32[]{:S(2)}, u32[]{:S(2)}) collective-permute-start(bf16[128,1024]{0,1:T(8,128)(2,1)S(1)} %collective-permute-done.12), channel_id=1, source_target_pairs={{1,0},{2,1},{3,2},{4,3},{5,4},{6,5},{7,6},{8,7},{9,8},{10,9},{11,1... | collective-permute-start | bytes 786440 | tf_op jit(solution)/shard_map/ppermute | solution.py:29
  191.5 4.3 collective-permute-done.6
  195.8 5.3 %collective-permute-start.14 = (bf16[128,1024]{0,1:T(8,128)(2,1)S(1)}, bf16[128,1024]{0,1:T(8,128)(2,1)S(1)}, u32[]{:S(2)}, u32[]{:S(2)}) collective-permute-start(bf16[128,1024]{0,1:T(8,128)(2,1)S(1)} %collective-permute-done.13), channel_id=1, source_target_pairs={{1,0},{2,1},{3,2},{4,3},{5,4},{6,5},{7,6},{8,7},{9,8},{10,9},{11,1... | collective-permute-start | bytes 786440 | tf_op jit(solution)/shard_map/ppermute | solution.py:29
  201.2 4.3 collective-permute-done.7
  205.5 5.4 %collective-permute-start.15 = (bf16[128,1024]{0,1:T(8,128)(2,1)S(1)}, bf16[128,1024]{0,1:T(8,128)(2,1)S(1)}, u32[]{:S(2)}, u32[]{:S(2)}) collective-permute-start(bf16[128,1024]{0,1:T(8,128)(2,1)S(1)} %collective-permute-done.14), channel_id=1, source_target_pairs={{1,0},{2,1},{3,2},{4,3},{5,4},{6,5},{7,6},{8,7},{9,8},{10,9},{11,1... | collective-permute-start | bytes 786440 | tf_op jit(solution)/shard_map/ppermute | solution.py:29
  210.9 5.2 %collective-permute-done.8 = bf16[128,1024]{0,1:T(8,128)(2,1)S(1)} collective-permute-done((bf16[128,1024]{0,1:T(8,128)(2,1)S(1)}, bf16[128,1024]{0,1:T(8,128)(2,1)S(1)}, u32[]{:S(2)}, u32[]{:S(2)}) %collective-permute-start.8) | collective-permute-done | bytes 262176 | tf_op jit(solution)/shard_map/ppermute | solution.py:27
  216.1 5.9 %collective-permute-start.16 = (bf16[128,1024]{0,1:T(8,128)(2,1)S(1)}, bf16[128,1024]{0,1:T(8,128)(2,1)S(1)}, u32[]{:S(2)}, u32[]{:S(2)}) collective-permute-start(bf16[128,1024]{0,1:T(8,128)(2,1)S(1)} %collective-permute-done.15), channel_id=1, source_target_pairs={{1,0},{2,1},{3,2},{4,3},{5,4},{6,5},{7,6},{8,7},{9,8},{10,9},{11,1... | collective-permute-start | bytes 786440 | tf_op jit(solution)/shard_map/ppermute | solution.py:29
  222.0 5.9 %collective-permute-done.9 = bf16[128,1024]{0,1:T(8,128)(2,1)S(1)} collective-permute-done((bf16[128,1024]{0,1:T(8,128)(2,1)S(1)}, bf16[128,1024]{0,1:T(8,128)(2,1)S(1)}, u32[]{:S(2)}, u32[]{:S(2)}) %collective-permute-start.9) | collective-permute-done | bytes 262176 | tf_op jit(solution)/shard_map/ppermute | solution.py:27
  230.5 5.4 %collective-permute-start.17 = (bf16[128,1024]{0,1:T(8,128)(2,1)S(1)}, bf16[128,1024]{0,1:T(8,128)(2,1)S(1)}, u32[]{:S(2)}, u32[]{:S(2)}) collective-permute-start(bf16[128,1024]{0,1:T(8,128)(2,1)S(1)} %collective-permute-done.16), channel_id=1, source_target_pairs={{1,0},{2,1},{3,2},{4,3},{5,4},{6,5},{7,6},{8,7},{9,8},{10,9},{11,1... | collective-permute-start | bytes 786440 | tf_op jit(solution)/shard_map/ppermute | solution.py:29
  235.9 4.5 collective-permute-done.10
  242.1 5.4 %collective-permute-start.18 = (bf16[128,1024]{0,1:T(8,128)(2,1)S(1)}, bf16[128,1024]{0,1:T(8,128)(2,1)S(1)}, u32[]{:S(2)}, u32[]{:S(2)}) collective-permute-start(bf16[128,1024]{0,1:T(8,128)(2,1)S(1)} %collective-permute-done.17), channel_id=1, source_target_pairs={{1,0},{2,1},{3,2},{4,3},{5,4},{6,5},{7,6},{8,7},{9,8},{10,9},{11,1... | collective-permute-start | bytes 786440 | tf_op jit(solution)/shard_map/ppermute | solution.py:29
  247.5 2.8 collective-permute-done.11
  263.8 5.2 %gather_fusion = bf16[16,128,1024]{1,2,0:T(8,128)(2,1)} fusion(bf16[16,128,1024]{1,2,0:T(8,128)(2,1)} %bitcast_dynamic-update-slice_fusion, s32[1024]{0:T(1024)S(1)} %pad_clamp_fusion), kind=kCustom, calls=%fused_computation | custom fusion | bytes 8388672 | tf_op jit(solution)/shard_map/gather | solution.py:33
  269.0 7.8 %bitcast_add_fusion = f32[1024,1024]{0,1:T(8,128)S(1)} fusion(bf16[16,128,1024]{1,2,0:T(8,128)(2,1)} %gather_fusion, f32[1024]{0:T(1024)S(1)} %fusion.84), kind=kOutput, calls=%fused_computation.5 | convolution fusion | flops 4298113024 | bytes 8392704 | tf_op jit(solution)/shard_map/dot_general | solution.py:132
  279.7 11.7 %cholesky.134 = f32[128,128]{1,0:T(8,128)S(1)} custom-call(f32[128,128]{1,0:T(8,128)S(1)} %fusion.81), custom_call_target="Cholesky" | custom-call | tf_op jit(solution)/shard_map/jit(cholesky)/cholesky | solution.py:69
  292.7 9.8 %custom-call.12 = f32[1,128,128]{1,2,0:T(8,128)S(1)} custom-call(f32[1,128,128]{2,1,0:T(8,128)S(1)} %fusion.44), custom_call_target="InvertDiagBlocksLowerTriangular" | custom-call | tf_op jit(solution)/shard_map/triangular_solve/custom-call.0 | solution.py:70
  306.1 4.6 slice_subtract_fusion
  312.9 12.7 %cholesky.145 = f32[128,128]{1,0:T(8,128)S(1)} custom-call(f32[128,128]{1,0:T(8,128)} %fusion.79), custom_call_target="Cholesky" | custom-call | tf_op jit(solution)/shard_map/jit(cholesky)/cholesky | solution.py:69
  327.5 11.3 %custom-call.13 = f32[1,128,128]{1,2,0:T(8,128)} custom-call(f32[1,128,128]{2,1,0:T(8,128)} %fusion.45), custom_call_target="InvertDiagBlocksLowerTriangular" | custom-call | tf_op jit(solution)/shard_map/triangular_solve/custom-call.0 | solution.py:70
  340.7 2.0 slice_subtract_fusion.1
  345.2 11.7 %cholesky.156 = f32[128,128]{1,0:T(8,128)S(1)} custom-call(f32[128,128]{1,0:T(8,128)S(1)} %fusion.77), custom_call_target="Cholesky" | custom-call | tf_op jit(solution)/shard_map/jit(cholesky)/cholesky | solution.py:69
  358.3 10.2 %custom-call.14 = f32[1,128,128]{1,2,0:T(8,128)S(1)} custom-call(f32[1,128,128]{2,1,0:T(8,128)S(1)} %fusion.46), custom_call_target="InvertDiagBlocksLowerTriangular" | custom-call | tf_op jit(solution)/shard_map/triangular_solve/custom-call.0 | solution.py:70
  370.5 2.9 slice_subtract_fusion.2
  373.5 11.7 %cholesky.167 = f32[128,128]{1,0:T(8,128)S(1)} custom-call(f32[128,128]{1,0:T(8,128)S(1)} %fusion.75), custom_call_target="Cholesky" | custom-call | tf_op jit(solution)/shard_map/jit(cholesky)/cholesky | solution.py:69
  386.5 9.8 %custom-call.15 = f32[1,128,128]{1,2,0:T(8,128)S(1)} custom-call(f32[1,128,128]{2,1,0:T(8,128)S(1)} %fusion.47), custom_call_target="InvertDiagBlocksLowerTriangular" | custom-call | tf_op jit(solution)/shard_map/triangular_solve/custom-call.0 | solution.py:70
  400.2 11.9 %cholesky.178 = f32[128,128]{1,0:T(8,128)S(1)} custom-call(f32[128,128]{1,0:T(8,128)S(1)} %fusion.73), custom_call_target="Cholesky" | custom-call | tf_op jit(solution)/shard_map/jit(cholesky)/cholesky | solution.py:69
  413.4 9.8 %custom-call.16 = f32[1,128,128]{1,2,0:T(8,128)S(1)} custom-call(f32[1,128,128]{2,1,0:T(8,128)S(1)} %fusion.48), custom_call_target="InvertDiagBlocksLowerTriangular" | custom-call | tf_op jit(solution)/shard_map/triangular_solve/custom-call.0 | solution.py:70
  426.8 11.7 %cholesky.189 = f32[128,128]{1,0:T(8,128)S(1)} custom-call(f32[128,128]{1,0:T(8,128)S(1)} %fusion.71), custom_call_target="Cholesky" | custom-call | tf_op jit(solution)/shard_map/jit(cholesky)/cholesky | solution.py:69
  439.7 9.8 %custom-call.17 = f32[1,128,128]{1,2,0:T(8,128)S(1)} custom-call(f32[1,128,128]{2,1,0:T(8,128)S(1)} %fusion.49), custom_call_target="InvertDiagBlocksLowerTriangular" | custom-call | tf_op jit(solution)/shard_map/triangular_solve/custom-call.0 | solution.py:70
  450.9 11.7 %cholesky.200 = f32[128,128]{1,0:T(8,128)S(1)} custom-call(f32[128,128]{1,0:T(8,128)S(1)} %fusion.69), custom_call_target="Cholesky" | custom-call | tf_op jit(solution)/shard_map/jit(cholesky)/cholesky | solution.py:69
  463.9 9.8 %custom-call.18 = f32[1,128,128]{1,2,0:T(8,128)S(1)} custom-call(f32[1,128,128]{2,1,0:T(8,128)S(1)} %fusion.50), custom_call_target="InvertDiagBlocksLowerTriangular" | custom-call | tf_op jit(solution)/shard_map/triangular_solve/custom-call.0 | solution.py:70
  483.0 12.0 %cholesky.211 = f32[128,128]{1,0:T(8,128)S(1)} custom-call(f32[128,128]{1,0:T(8,128)S(1)} %fusion.67), custom_call_target="Cholesky" | custom-call | tf_op jit(solution)/shard_map/jit(cholesky)/cholesky | solution.py:69
  496.3 9.8 %custom-call.19 = f32[1,128,128]{1,2,0:T(8,128)S(1)} custom-call(f32[1,128,128]{2,1,0:T(8,128)S(1)} %fusion.51), custom_call_target="InvertDiagBlocksLowerTriangular" | custom-call | tf_op jit(solution)/shard_map/triangular_solve/custom-call.0 | solution.py:70
  (174 shorter events, 75.4 us)
Async XLA Ops:
  6.5 158.5 %reduce-scatter.2.cloned.1.call-start = ((), (), s32[]{:S(2)}) async-start(), calls=%async_computation.1 | async-start | bytes 8912896 | tf_op jit(solution)/shard_map/reduce_scatter | solution.py:125
  16.8 1.9 copy-start
  18.8 8.0 %copy-start.15 = (f32[2,8,128]{2,1,0:T(8,128)S(1)}, f32[2,8,128]{2,1,0:T(8,128)}, u32[]{:S(2)}) copy-start(f32[2,8,128]{2,1,0:T(8,128)} %param.13) | copy-start | bytes 24580
  19.0 7.9 %collective-permute-start.1 = (bf16[128,4,512]{2,0,1:T(8,128)(2,1)S(1)}, bf16[128,4,512]{2,0,1:T(8,128)(2,1)S(1)}, u32[]{:S(2)}, u32[]{:S(2)}) collective-permute-start(bf16[128,4,512]{2,0,1:T(8,128)(2,1)S(1)} %get-tuple-element.13), channel_id=1, source_target_pairs={{16,0},{32,16},{48,32},{64,48},{80,64},{96,80},{112,96},{17,1},{33... | collective-permute-start | bytes 1572872 | tf_op jit(solution)/shard_map/ppermute | solution.py:41
  20.3 6.6 %collective-permute-start.3 = (bf16[128,4,512]{2,0,1:T(8,128)(2,1)S(1)}, bf16[128,4,512]{2,0,1:T(8,128)(2,1)S(1)}, u32[]{:S(2)}, u32[]{:S(2)}) collective-permute-start(bf16[128,4,512]{2,0,1:T(8,128)(2,1)S(1)} %get-tuple-element.14), channel_id=1, source_target_pairs={{0,16},{16,32},{32,48},{48,64},{64,80},{80,96},{96,112},{1,17},{17... | collective-permute-start | bytes 1572872 | tf_op jit(solution)/shard_map/ppermute | solution.py:41
  25.3 11.2 %copy-start.1 = (bf16[1024,4,512]{2,0,1:T(8,128)(2,1)S(1)}, bf16[1024,4,512]{2,0,1:T(8,128)(2,1)}, u32[]{:S(2)}) copy-start(bf16[1024,4,512]{2,0,1:T(8,128)(2,1)} %copy-done) | copy-start | bytes 12582916
  28.8 11.5 %collective-permute-start = (bf16[128,4,512]{2,0,1:T(8,128)(2,1)S(1)}, bf16[128,4,512]{2,0,1:T(8,128)(2,1)S(1)}, u32[]{:S(2)}, u32[]{:S(2)}) collective-permute-start(bf16[128,4,512]{2,0,1:T(8,128)(2,1)S(1)} %get-tuple-element.12), channel_id=1, source_target_pairs={{16,0},{32,16},{48,32},{64,48},{80,64},{96,80},{112,96},{17,1},{33... | collective-permute-start | bytes 1572872 | tf_op jit(solution)/shard_map/ppermute | solution.py:41
  30.1 21.7 %collective-permute-start.2 = (bf16[128,4,512]{2,0,1:T(8,128)(2,1)S(1)}, bf16[128,4,512]{2,0,1:T(8,128)(2,1)S(1)}, u32[]{:S(2)}, u32[]{:S(2)}) collective-permute-start(bf16[128,4,512]{2,0,1:T(8,128)(2,1)S(1)} %get-tuple-element.10), channel_id=1, source_target_pairs={{0,16},{16,32},{32,48},{48,64},{64,80},{80,96},{96,112},{1,17},{17... | collective-permute-start | bytes 1572872 | tf_op jit(solution)/shard_map/ppermute | solution.py:41
  74.0 153.9 %copy-start.16 = (s32[8]{0:T(128)S(1)}, s32[8]{0:T(128)}, u32[]{:S(2)}) copy-start(s32[8]{0:T(128)} %param.14) | copy-start | bytes 100
  165.1 92.9 %copy-start.7 = (f32[128,1024]{0,1:T(8,128)S(1)}, f32[128,1024]{0,1:T(8,128)}, u32[]{:S(2)}) copy-start(f32[128,1024]{0,1:T(8,128)} %reduce-scatter.2.cloned.1.call-done) | copy-start | bytes 1572868
  166.2 10.2 %collective-permute-start.4 = (bf16[128,1024]{0,1:T(8,128)(2,1)S(1)}, bf16[128,1024]{0,1:T(8,128)(2,1)S(1)}, u32[]{:S(2)}, u32[]{:S(2)}) collective-permute-start(bf16[128,1024]{0,1:T(8,128)(2,1)S(1)} %convert_element_type.87), channel_id=1, source_target_pairs={{0,1},{1,2},{2,3},{3,4},{4,5},{5,6},{6,7},{7,8},{8,9},{9,10},{10,1... | collective-permute-start | bytes 786440 | tf_op jit(solution)/shard_map/ppermute | solution.py:27
  176.4 9.7 %collective-permute-start.5 = (bf16[128,1024]{0,1:T(8,128)(2,1)S(1)}, bf16[128,1024]{0,1:T(8,128)(2,1)S(1)}, u32[]{:S(2)}, u32[]{:S(2)}) collective-permute-start(bf16[128,1024]{0,1:T(8,128)(2,1)S(1)} %collective-permute-done.4), channel_id=1, source_target_pairs={{0,1},{1,2},{2,3},{3,4},{4,5},{5,6},{6,7},{7,8},{8,9},{9,10},{10,1... | collective-permute-start | bytes 786440 | tf_op jit(solution)/shard_map/ppermute | solution.py:27
  176.4 9.7 %collective-permute-start.12 = (bf16[128,1024]{0,1:T(8,128)(2,1)S(1)}, bf16[128,1024]{0,1:T(8,128)(2,1)S(1)}, u32[]{:S(2)}, u32[]{:S(2)}) collective-permute-start(bf16[128,1024]{0,1:T(8,128)(2,1)S(1)} %convert_element_type.87), channel_id=1, source_target_pairs={{1,0},{2,1},{3,2},{4,3},{5,4},{6,5},{7,6},{8,7},{9,8},{10,9},{11,1... | collective-permute-start | bytes 786440 | tf_op jit(solution)/shard_map/ppermute | solution.py:29
  186.1 9.7 %collective-permute-start.6 = (bf16[128,1024]{0,1:T(8,128)(2,1)S(1)}, bf16[128,1024]{0,1:T(8,128)(2,1)S(1)}, u32[]{:S(2)}, u32[]{:S(2)}) collective-permute-start(bf16[128,1024]{0,1:T(8,128)(2,1)S(1)} %collective-permute-done.5), channel_id=1, source_target_pairs={{0,1},{1,2},{2,3},{3,4},{4,5},{5,6},{6,7},{7,8},{8,9},{9,10},{10,1... | collective-permute-start | bytes 786440 | tf_op jit(solution)/shard_map/ppermute | solution.py:27
  186.1 9.7 %collective-permute-start.13 = (bf16[128,1024]{0,1:T(8,128)(2,1)S(1)}, bf16[128,1024]{0,1:T(8,128)(2,1)S(1)}, u32[]{:S(2)}, u32[]{:S(2)}) collective-permute-start(bf16[128,1024]{0,1:T(8,128)(2,1)S(1)} %collective-permute-done.12), channel_id=1, source_target_pairs={{1,0},{2,1},{3,2},{4,3},{5,4},{6,5},{7,6},{8,7},{9,8},{10,9},{11,1... | collective-permute-start | bytes 786440 | tf_op jit(solution)/shard_map/ppermute | solution.py:29
  195.8 9.7 %collective-permute-start.7 = (bf16[128,1024]{0,1:T(8,128)(2,1)S(1)}, bf16[128,1024]{0,1:T(8,128)(2,1)S(1)}, u32[]{:S(2)}, u32[]{:S(2)}) collective-permute-start(bf16[128,1024]{0,1:T(8,128)(2,1)S(1)} %collective-permute-done.6), channel_id=1, source_target_pairs={{0,1},{1,2},{2,3},{3,4},{4,5},{5,6},{6,7},{7,8},{8,9},{9,10},{10,1... | collective-permute-start | bytes 786440 | tf_op jit(solution)/shard_map/ppermute | solution.py:27
  195.8 9.7 %collective-permute-start.14 = (bf16[128,1024]{0,1:T(8,128)(2,1)S(1)}, bf16[128,1024]{0,1:T(8,128)(2,1)S(1)}, u32[]{:S(2)}, u32[]{:S(2)}) collective-permute-start(bf16[128,1024]{0,1:T(8,128)(2,1)S(1)} %collective-permute-done.13), channel_id=1, source_target_pairs={{1,0},{2,1},{3,2},{4,3},{5,4},{6,5},{7,6},{8,7},{9,8},{10,9},{11,1... | collective-permute-start | bytes 786440 | tf_op jit(solution)/shard_map/ppermute | solution.py:29
  205.5 10.6 %collective-permute-start.8 = (bf16[128,1024]{0,1:T(8,128)(2,1)S(1)}, bf16[128,1024]{0,1:T(8,128)(2,1)S(1)}, u32[]{:S(2)}, u32[]{:S(2)}) collective-permute-start(bf16[128,1024]{0,1:T(8,128)(2,1)S(1)} %collective-permute-done.7), channel_id=1, source_target_pairs={{0,1},{1,2},{2,3},{3,4},{4,5},{5,6},{6,7},{7,8},{8,9},{9,10},{10,1... | collective-permute-start | bytes 786440 | tf_op jit(solution)/shard_map/ppermute | solution.py:27
  205.5 10.6 %collective-permute-start.15 = (bf16[128,1024]{0,1:T(8,128)(2,1)S(1)}, bf16[128,1024]{0,1:T(8,128)(2,1)S(1)}, u32[]{:S(2)}, u32[]{:S(2)}) collective-permute-start(bf16[128,1024]{0,1:T(8,128)(2,1)S(1)} %collective-permute-done.14), channel_id=1, source_target_pairs={{1,0},{2,1},{3,2},{4,3},{5,4},{6,5},{7,6},{8,7},{9,8},{10,9},{11,1... | collective-permute-start | bytes 786440 | tf_op jit(solution)/shard_map/ppermute | solution.py:29
  216.1 11.8 %collective-permute-start.9 = (bf16[128,1024]{0,1:T(8,128)(2,1)S(1)}, bf16[128,1024]{0,1:T(8,128)(2,1)S(1)}, u32[]{:S(2)}, u32[]{:S(2)}) collective-permute-start(bf16[128,1024]{0,1:T(8,128)(2,1)S(1)} %collective-permute-done.8), channel_id=1, source_target_pairs={{0,1},{1,2},{2,3},{3,4},{4,5},{5,6},{6,7},{7,8},{8,9},{9,10},{10,1... | collective-permute-start | bytes 786440 | tf_op jit(solution)/shard_map/ppermute | solution.py:27
  216.1 14.3 %collective-permute-start.16 = (bf16[128,1024]{0,1:T(8,128)(2,1)S(1)}, bf16[128,1024]{0,1:T(8,128)(2,1)S(1)}, u32[]{:S(2)}, u32[]{:S(2)}) collective-permute-start(bf16[128,1024]{0,1:T(8,128)(2,1)S(1)} %collective-permute-done.15), channel_id=1, source_target_pairs={{1,0},{2,1},{3,2},{4,3},{5,4},{6,5},{7,6},{8,7},{9,8},{10,9},{11,1... | collective-permute-start | bytes 786440 | tf_op jit(solution)/shard_map/ppermute | solution.py:29
  227.9 12.5 %copy-start.14 = (bf16[128,1024]{0,1:T(8,128)(2,1)}, bf16[128,1024]{0,1:T(8,128)(2,1)S(1)}, u32[]{:S(2)}) copy-start(bf16[128,1024]{0,1:T(8,128)(2,1)S(1)} %collective-permute-done.9) | copy-start | bytes 786436
  227.9 12.5 %collective-permute-start.10 = (bf16[128,1024]{0,1:T(8,128)(2,1)S(1)}, bf16[128,1024]{0,1:T(8,128)(2,1)}, u32[]{:S(2)}, u32[]{:S(2)}) collective-permute-start(bf16[128,1024]{0,1:T(8,128)(2,1)S(1)} %collective-permute-done.9), channel_id=1, source_target_pairs={{0,1},{1,2},{2,3},{3,4},{4,5},{5,6},{6,7},{7,8},{8,9},{9,10},{10,1... | collective-permute-start | bytes 786440 | tf_op jit(solution)/shard_map/ppermute | solution.py:27
  230.5 11.6 %collective-permute-start.17 = (bf16[128,1024]{0,1:T(8,128)(2,1)S(1)}, bf16[128,1024]{0,1:T(8,128)(2,1)S(1)}, u32[]{:S(2)}, u32[]{:S(2)}) collective-permute-start(bf16[128,1024]{0,1:T(8,128)(2,1)S(1)} %collective-permute-done.16), channel_id=1, source_target_pairs={{1,0},{2,1},{3,2},{4,3},{5,4},{6,5},{7,6},{8,7},{9,8},{10,9},{11,1... | collective-permute-start | bytes 786440 | tf_op jit(solution)/shard_map/ppermute | solution.py:29
  240.4 9.9 %collective-permute-start.11 = (bf16[128,1024]{0,1:T(8,128)(2,1)}, bf16[128,1024]{0,1:T(8,128)(2,1)S(1)}, u32[]{:S(2)}, u32[]{:S(2)}) collective-permute-start(bf16[128,1024]{0,1:T(8,128)(2,1)} %collective-permute-done.10), channel_id=1, source_target_pairs={{0,1},{1,2},{2,3},{3,4},{4,5},{5,6},{6,7},{7,8},{8,9},{9,10},{10,1... | collective-permute-start | bytes 786440 | tf_op jit(solution)/shard_map/ppermute | solution.py:27
  242.1 20.9 %collective-permute-start.18 = (bf16[128,1024]{0,1:T(8,128)(2,1)S(1)}, bf16[128,1024]{0,1:T(8,128)(2,1)S(1)}, u32[]{:S(2)}, u32[]{:S(2)}) collective-permute-start(bf16[128,1024]{0,1:T(8,128)(2,1)S(1)} %collective-permute-done.17), channel_id=1, source_target_pairs={{1,0},{2,1},{3,2},{4,3},{5,4},{6,5},{7,6},{8,7},{9,8},{10,9},{11,1... | collective-permute-start | bytes 786440 | tf_op jit(solution)/shard_map/ppermute | solution.py:29
  276.8 1.9 copy-start.9
  302.8 0.6 copy-start.12
  305.4 0.8 copy-start.3
  340.7 2.1 copy-start.5
  342.8 1.4 copy-start.2
  368.8 28.4 %copy-start.10 = (f32[128,128]{1,0:T(8,128)}, f32[128,128]{1,0:T(8,128)S(1)}, u32[]{:S(2)}) copy-start(f32[128,128]{1,0:T(8,128)S(1)} %fusion.34) | copy-start | bytes 196612
  397.2 77.9 %copy-start.4 = (f32[896,128]{1,0:T(8,128)S(1)}, f32[896,128]{1,0:T(8,128)}, u32[]{:S(2)}) copy-start(f32[896,128]{1,0:T(8,128)} %copy-done.3) | copy-start | bytes 1376260
  398.2 1.0 copy-start.8
  399.2 75.1 %copy-start.13 = (f32[128,128]{1,0:T(8,128)S(1)}, f32[128,128]{1,0:T(8,128)}, u32[]{:S(2)}) copy-start(f32[128,128]{1,0:T(8,128)} %copy-done.12) | copy-start | bytes 196612
  399.2 77.2 %copy-start.6 = (f32[768,128]{1,0:T(8,128)S(1)}, f32[768,128]{1,0:T(8,128)}, u32[]{:S(2)}) copy-start(f32[768,128]{1,0:T(8,128)} %copy-done.5) | copy-start | bytes 1179652
  399.3 77.6 %copy-start.11 = (f32[128,128]{1,0:T(8,128)S(1)}, f32[128,128]{1,0:T(8,128)}, u32[]{:S(2)}) copy-start(f32[128,128]{1,0:T(8,128)} %copy-done.10) | copy-start | bytes 196612
Sparse Core Ops, SparseCore 0:
  74.1 90.8 reduce-scatter.1
